TPU v7x, 128 devices: a whole 4x4x4 slice. The times are simulated.
128 devices in a mesh: runs: 32 (over x, z, y_hi), chan: 4 (over y_lo, core).
Axes of the slice: x: 4, y: 4 (y_hi: 2, y_lo: 2; y = y_hi * 2 + y_lo), z: 4, core: 2. Of those that a mesh axis runs over, the one named last changes fastest.
Arguments:
- slices: bfloat16 [256, 512, 8192], P('runs', None, 'chan'), may hold values from -6 to 6
- spectra: bfloat16 [2, 48, 8192], P(None, None, 'chan'), may hold values from -0.0625 to 0.0625
- loadings: float32 [256, 48], replicated, may hold values from 0.5 to 2
- mixing: float32 [2, 48, 48], replicated, may hold values from -1 to 3.5
- halves: int32 [256], replicated, may hold values from 0 to 1, as said below
- partner: int32 [256], replicated, may hold values from 0 to 255, as said below
Outputs:
- new_spectra: float32 [2, 48, 8192], P(None, None, 'chan')
- held_residual: float32 [256, 48, 8192], P('runs', None, 'chan')
Inputs may be any that keep to these rules, and one draw needn't show every extreme that they name: `halves`: exactly half of the 256 runs are in each half. partner pairs every run with a run of the other half, and the partner of a run's partner is the run itself.
All inputs are finite; a program needn't handle non-finite values.
Results may differ from a plain program's by a relative error of at most 0.0045.
Values may be sent and summed in bfloat16 or wider, within the bound.
No kernel may reach another device: no remote copies, remote signals or barrier semaphores. Data moves between devices by JAX's collectives and lax.ppermute only.
A program may use at most 64 MiB of HBM per device.

v0:
```python
import jax
import jax.numpy as jnp
from jax import lax
from jax.sharding import PartitionSpec as P

NS_STEPS = 10


def polar_scale(gram):
    eye_rank = jnp.eye(gram.shape[-1], dtype=jnp.float32)
    traces = jnp.trace(gram, axis1=1, axis2=2)
    start = eye_rank[None] / jnp.sqrt(traces + 1e-06)[:, None, None]

    def advance(step, factor):
        left = jnp.einsum("nrs,nrt->nst", factor, gram, precision=lax.Precision.HIGHEST)
        inner = jnp.einsum("nst,ntu->nsu", left, factor, precision=lax.Precision.HIGHEST)
        return 0.5 * jnp.einsum(
            "nrs,nsu->nru", factor, 3.0 * eye_rank[None] - inner, precision=lax.Precision.HIGHEST
        )

    return lax.fori_loop(0, NS_STEPS, advance, start)


def project(slices, rows_low, mixed):
    partial_basis = jnp.einsum("nrj,nij->nri", rows_low, slices, preferred_element_type=jnp.float32)
    basis = lax.psum(partial_basis, "chan")
    scaled = jnp.einsum("nrs,nsi->nri", mixed, basis, precision=lax.Precision.HIGHEST)
    gram = jnp.einsum("nri,nsi->nrs", scaled, scaled, precision=lax.Precision.HIGHEST)
    factor = polar_scale(gram)
    rotated = jnp.einsum("nrs,nri->nsi", factor, scaled, precision=lax.Precision.HIGHEST).astype(
        jnp.bfloat16
    )
    result = jnp.einsum("nsi,nij->nsj", rotated, slices, preferred_element_type=jnp.float32)
    return result


def solve_one(lower, target):
    return jax.scipy.linalg.cho_solve((lower, True), target)


def solve_halves(system, moments):
    lower = jnp.linalg.cholesky(system)
    return jax.vmap(solve_one)(lower, moments)


def body(slices, spectra, loadings, mixing, halves, partner):
    run_count = slices.shape[0]
    total_runs = loadings.shape[0]
    first_run = lax.axis_index("runs") * run_count
    mine = first_run + jnp.arange(run_count, dtype=jnp.int32)
    all_runs = jnp.arange(total_runs, dtype=jnp.int32)
    matches = all_runs[None, :] == mine[:, None]
    my_halves = jnp.sum(jnp.where(matches, halves[None, :], 0), axis=1)
    my_mates = jnp.sum(jnp.where(matches, partner[None, :], 0), axis=1)
    my_loads = jnp.dot(matches.astype(jnp.float32), loadings, precision=lax.Precision.HIGHEST)
    mate_match = (all_runs[None, :] == my_mates[:, None]).astype(jnp.float32)
    mate_loads = jnp.dot(mate_match, loadings, precision=lax.Precision.HIGHEST)
    first_half = (my_halves == 0)[:, None, None]
    own_rows = jnp.where(first_half, spectra[0][None], spectra[1][None])
    own_mix = jnp.where(first_half, mixing[0][None], mixing[1][None]) * my_loads[:, None, :]
    projected = project(slices, own_rows, own_mix)
    terms = jnp.einsum("nsr,nsj->nrj", own_mix, projected, precision=lax.Precision.HIGHEST)
    mine_member = (my_halves[:, None] == jnp.arange(2, dtype=jnp.int32)[None, :]).astype(
        jnp.float32
    )
    partial_moments = jnp.einsum("nh,nrj->hrj", mine_member, terms, precision=lax.Precision.HIGHEST)
    member = (halves[:, None] == jnp.arange(2, dtype=jnp.int32)[None, :]).astype(jnp.float32)
    cross = jnp.einsum("kh,kr,ks->hrs", member, loadings, loadings, precision=lax.Precision.HIGHEST)
    inner_mix = jnp.einsum("hsr,hst->hrt", mixing, mixing, precision=lax.Precision.HIGHEST)
    system = inner_mix * cross
    moments = lax.psum(partial_moments, "runs")
    new_spectra = solve_halves(system, moments)
    held_rows = jnp.where(first_half, new_spectra[1][None], new_spectra[0][None])
    held_mix = jnp.where(first_half, mixing[1][None], mixing[0][None]) * mate_loads[:, None, :]
    held_projected = project(slices, held_rows.astype(jnp.bfloat16), held_mix)
    model_part = jnp.einsum("nrs,nsj->nrj", held_mix, held_rows, precision=lax.Precision.HIGHEST)
    return (new_spectra, held_projected - model_part)


def solution(mesh):
    placed = (P("runs", None, "chan"), P(None, None, "chan"), P(), P(), P(), P())
    return jax.shard_map(
        body,
        mesh=mesh,
        in_specs=placed,
        out_specs=(P(None, None, "chan"), P("runs", None, "chan")),
        check_vma=False,
    )
```

profile of v0, /device:TPU:1, one launch (start us, length us, event | category | flops | bytes accessed | tf_op | source)
XLA Modules:
  0.0 539.7 jit_solution(11662439572653921339)
XLA Ops:
  7.2 0.9 select_reduce_fusion.3
  8.1 1.1 slice_bitcast_fusion.3
  9.2 11.9 %fusion.17 = f32[8,48,512]{2,1,0:T(8,128)} fusion(bf16[8,512,2048]{2,1,0:T(8,128)(2,1)} %param.10, pred[8]{0:T(512)(128)(4,1)S(1)} %broadcast_compare_fusion, bf16[48,2048]{1,0:T(8,128)(2,1)S(1)} %get-tuple-element.81, bf16[48,2048]{1,0:T(8,128)(2,1)S(1)} %get-tuple-element.80), kind=kOutput, calls=%fused_computation.23 | convolution fusion | flops 806092800 | bytes 17956872 | tf_op jit(solution)/shard_map/nrj,nij->nri/dot_general | solution.py:25
  22.1 42.1 %all-reduce.4.cloned.1.call-done = f32[8,48,512]{2,1,0:T(8,128)} async-done(((f32[8,48,512]{2,1,0:T(8,128)}), f32[8,48,512]{2,1,0:T(8,128)}) %all-reduce.4.cloned.1.call-update) | async-done | bytes 786448 | tf_op jit(solution)/shard_map/psum | solution.py:26
  64.3 2.0 fusion.26
  66.2 0.9 select_reduce_fusion.1
  67.3 11.6 %while.22 = (s32[]{:T(128)}, f32[8,48,48]{1,2,0:T(8,128)S(1)}, f32[8,48,48]{2,1,0:T(8,128)S(1)}, s32[]{:T(128)}) while((s32[]{:T(128)}, f32[8,48,48]{1,2,0:T(8,128)S(1)}, f32[8,48,48]{2,1,0:T(8,128)S(1)}, s32[]{:T(128)}) %tuple.47), condition=%wide.region_6.7_spmd.clone, body=%wide.region_5.6_spmd.clone.sunk | while | flops 31891968 | bytes 829493 | solution.py:21
  67.5 0.3 fusion.126
  67.8 0.4 convolution_subtract_fusion.5
  68.6 0.3 fusion.126
  69.0 0.4 convolution_subtract_fusion.5
  69.8 0.3 fusion.126
  70.1 0.4 convolution_subtract_fusion.5
  70.9 0.3 fusion.126
  71.3 0.4 convolution_subtract_fusion.5
  72.1 0.3 fusion.126
  72.4 0.4 convolution_subtract_fusion.5
  73.2 0.3 fusion.126
  73.6 0.4 convolution_subtract_fusion.5
  74.4 0.3 fusion.126
  74.7 0.4 convolution_subtract_fusion.5
  75.5 0.3 fusion.126
  75.8 0.4 convolution_subtract_fusion.5
  76.6 0.3 fusion.126
  77.0 0.4 convolution_subtract_fusion.5
  77.8 0.3 fusion.126
  78.1 0.4 convolution_subtract_fusion.5
  78.9 0.8 convolution_convert_fusion.1
  79.7 8.8 %fusion.66 = f32[8,48,2048]{2,1,0:T(8,128)S(1)} fusion(bf16[8,48,512]{2,1,0:T(8,128)(2,1)S(1)} %convolution_convert_fusion.1, bf16[8,512,2048]{2,1,0:T(8,128)(2,1)} %param.10), kind=kOutput, calls=%fused_computation.102 | convolution fusion | flops 805306368 | bytes 20316160 | tf_op jit(solution)/shard_map/nsi,nij->nsj/dot_general | solution.py:33
  88.5 3.1 fusion.25
  91.6 3.3 fusion.10
  94.9 1.3 copy.24
  96.4 9.0 %custom-call.11 = f32[2,48,48]{2,1,0:T(8,128)S(1)} custom-call(f32[2,48,48]{2,1,0:T(8,128)S(1)} %fusion.51), custom_call_target="Cholesky" | custom-call | tf_op jit(solution)/shard_map/jit(cholesky)/cholesky | solution.py:42
  105.6 7.4 %custom-call.12 = f32[2,1,48,48]{2,3,1,0:T(8,128)S(1)} custom-call(f32[2,1,48,48]{3,2,1,0:T(8,128)S(1)} %select_bitcast_fusion), custom_call_target="InvertDiagBlocksLowerTriangular" | custom-call | tf_op jit(solution)/shard_map/vmap(jit(_cho_solve))/triangular_solve | solution.py:38
  113.0 315.1 %all-reduce.6.cloned.1.call-done = f32[2,48,2048]{2,1,0:T(8,128)} async-done(((f32[2,48,2048]{2,1,0:T(8,128)}), f32[2,48,2048]{2,1,0:T(8,128)}) %all-reduce.6.cloned.1.call-update) | async-done | bytes 786448 | tf_op jit(solution)/shard_map/psum | solution.py:71
  428.1 2.0 fusion.48
  430.1 0.8 fusion.46
  431.0 12.1 %fusion.12 = f32[8,48,512]{2,1,0:T(8,128)} fusion(bf16[8,512,2048]{2,1,0:T(8,128)(2,1)} %param.10, f32[48,2048]{1,0:T(8,128)S(1)} %get-tuple-element.79, f32[48,2048]{1,0:T(8,128)S(1)} %get-tuple-element.78, pred[8]{0:T(512)(128)(4,1)S(1)} %broadcast_compare_fusion), kind=kOutput, calls=%fused_computation.18 | convolution fusion | flops 806092800 | bytes 18350088 | tf_op jit(solution)/shard_map/nrj,nij->nri/dot_general | solution.py:25
  443.2 4.5 fusion.8
  447.7 58.4 %all-reduce.8.cloned.1.call-done = f32[8,48,512]{2,1,0:T(8,128)} async-done(((f32[8,48,512]{2,1,0:T(8,128)}), f32[8,48,512]{2,1,0:T(8,128)}) %all-reduce.8.cloned.1.call-update) | async-done | bytes 786448 | tf_op jit(solution)/shard_map/psum | solution.py:26
  506.1 2.0 fusion.24
  508.1 0.9 select_reduce_fusion
  509.2 11.7 %while.23 = (s32[]{:T(128)}, f32[8,48,48]{1,2,0:T(8,128)S(1)}, f32[8,48,48]{2,1,0:T(8,128)S(1)}, s32[]{:T(128)}) while((s32[]{:T(128)}, f32[8,48,48]{1,2,0:T(8,128)S(1)}, f32[8,48,48]{2,1,0:T(8,128)S(1)}, s32[]{:T(128)}) %tuple.50), condition=%wide.region_12.13_spmd.clone, body=%wide.region_11.12_spmd.clone.sunk | while | flops 31891968 | bytes 829493 | solution.py:21
  509.2 0.3 fusion.135
  509.5 0.4 convolution_subtract_fusion.6
  510.3 0.3 fusion.135
  510.7 0.4 convolution_subtract_fusion.6
  511.5 0.3 fusion.135
  511.8 0.4 convolution_subtract_fusion.6
  512.6 0.3 fusion.135
  513.0 0.4 convolution_subtract_fusion.6
  513.8 0.3 fusion.135
  514.1 0.4 convolution_subtract_fusion.6
  514.9 0.3 fusion.135
  515.3 0.4 convolution_subtract_fusion.6
  516.1 0.3 fusion.135
  516.4 0.4 convolution_subtract_fusion.6
  517.2 0.3 fusion.135
  517.6 0.4 convolution_subtract_fusion.6
  518.4 0.3 fusion.135
  518.7 0.4 convolution_subtract_fusion.6
  519.8 0.4 convolution_subtract_fusion.6
  520.9 0.8 convolution_convert_fusion
  521.7 11.5 %convolution_subtract_fusion.2 = f32[8,48,2048]{2,1,0:T(8,128)} fusion(f32[8,48,2048]{2,1,0:T(8,128)} %fusion.8, bf16[8,48,512]{2,1,0:T(8,128)(2,1)S(1)} %convolution_convert_fusion, bf16[8,512,2048]{2,1,0:T(8,128)(2,1)} %param.10), kind=kOutput, calls=%fused_computation.17 | convolution fusion | flops 806092800 | bytes 23461888 | tf_op jit(solution)/shard_map/nsi,nij->nsj/dot_general | solution.py:33
  (98 shorter events, 8.9 us)
Async XLA Ops:
  7.2 57.1 %all-reduce.4.cloned.1.call-start = ((), (), s32[]{:S(2)}) async-start(), calls=%async_computation | async-start | bytes 1572864 | tf_op jit(solution)/shard_map/psum | solution.py:26
  9.2 12.0 %copy-start.3 = (s32[256]{0:T(256)S(1)}, s32[256]{0:T(256)}, u32[]{:S(2)}) copy-start(s32[256]{0:T(256)} %param.14) | copy-start | bytes 3076
  9.2 12.1 %copy-start.2 = (f32[256,48]{0,1:T(8,128)S(1)}, f32[256,48]{0,1:T(8,128)}, u32[]{:S(2)}) copy-start(f32[256,48]{0,1:T(8,128)} %param.12) | copy-start | bytes 147460
  9.2 12.4 %copy-start.1 = (f32[2,48,48]{2,1,0:T(8,128)S(1)}, f32[2,48,48]{2,1,0:T(8,128)}, u32[]{:S(2)}) copy-start(f32[2,48,48]{2,1,0:T(8,128)} %param.13) | copy-start | bytes 55300
  21.1 407.0 %all-reduce.6.cloned.1.call-start = ((), (), s32[]{:S(2)}) async-start(), calls=%async_computation.1 | async-start | bytes 1572864 | tf_op jit(solution)/shard_map/psum | solution.py:71
  96.3 409.9 %all-reduce.8.cloned.1.call-start = ((), (), s32[]{:S(2)}) async-start(), calls=%async_computation.2 | async-start | bytes 1572864 | tf_op jit(solution)/shard_map/psum | solution.py:26
  430.9 12.1 %copy-start = (f32[2,48,2048]{2,1,0:T(8,128)}, f32[2,48,2048]{2,1,0:T(8,128)S(1)}, u32[]{:S(2)}) copy-start(f32[2,48,2048]{2,1,0:T(8,128)S(1)} %fusion.46) | copy-start | bytes 2359300
Sparse Core Ops, SparseCore 0:
  21.2 42.9 all-reduce.3
  96.4 331.6 all-reduce.5
  443.2 62.9 all-reduce.7
where the time goes:
time: 540 us
  waiting for transfers between devices  416 us (77%)
  matrix products  87.5 us (16%)
  other arithmetic  17.9 us (3%)
  between operations  14 us (3%)
    psum x1, waiting for transfers between devices, body(): moments = lax.psum(partial_moments, 'runs')  315 us
    psum x2, waiting for transfers between devices, project(): basis = lax.psum(partial_basis, 'chan')  101 us
    dot_general x2, matrix products, project(): jnp.einsum('nrj,nij->nri', rows_low, slices, preferred_element_type=jnp.f...  23.9 us
    dot_general x2, matrix products, project(): jnp.einsum('nsi,nij->nsj', rotated, slices, preferred_element_type=jnp.fl...  20.3 us
  transfers between devices with their start and end apart: 3, of which 3 were waited for; matrix products, arithmetic and copies ran while one was open for 4% of the time, Pallas kernels for 0%

commit v1 on v0

--- a/solution.py
+++ b/solution.py
@@ -68,7 +68,11 @@
     cross = jnp.einsum("kh,kr,ks->hrs", member, loadings, loadings, precision=lax.Precision.HIGHEST)
     inner_mix = jnp.einsum("hsr,hst->hrt", mixing, mixing, precision=lax.Precision.HIGHEST)
     system = inner_mix * cross
-    moments = lax.psum(partial_moments, "runs")
+
+    def group_the_sections(x_part):
+        return lax.all_gather(x_part, "runs").sum(axis=0)
+
+    moments = group_the_sections(partial_moments)
     new_spectra = solve_halves(system, moments)
     held_rows = jnp.where(first_half, new_spectra[1][None], new_spectra[0][None])
     held_mix = jnp.where(first_half, mixing[1][None], mixing[0][None]) * mate_loads[:, None, :]

time: 540 us -> 402 us (0.74)
  waiting for transfers between devices: 416 us -> 266 us
  other arithmetic: 17.9 us -> 27 us
    psum x1 -> x0, waiting for transfers between devices: 315 us -> none  [body(): moments = lax.psum(partial_moments, 'runs')]
    all_gather x0 -> x1, waiting for transfers between devices: none -> 189 us  [group_the_sections(): return lax.all_gather(x_part, 'runs').sum(axis=0)]
    psum x2, waiting for transfers between devices: 101 us -> 76.6 us  [project(): basis = lax.psum(partial_basis, 'chan')]
    reduce_sum x0 -> x1, other arithmetic: none -> 9.05 us  [group_the_sections(): return lax.all_gather(x_part, 'runs').sum(axis=0)]
  transfers between devices with their start and end apart: 3 -> 3, of which waited for: 3 -> 3; matrix products, arithmetic and copies ran while one was open for 4% -> 6% of each run, Pallas kernels for 0% -> 0%
where the time goes in v1:
time: 402 us
  waiting for transfers between devices  266 us (66%)
  matrix products  89.9 us (22%)
  other arithmetic  27 us (7%)
  between operations  14 us (3%)
    all_gather x1, waiting for transfers between devices, group_the_sections(): return lax.all_gather(x_part, 'runs').sum(axis=0)  189 us
    psum x2, waiting for transfers between devices, project(): basis = lax.psum(partial_basis, 'chan')  76.6 us
    dot_general x2, matrix products, project(): jnp.einsum('nrj,nij->nri', rows_low, slices, preferred_element_type=jnp.f...  23.9 us
    dot_general x2, matrix products, project(): jnp.einsum('nsi,nij->nsj', rotated, slices, preferred_element_type=jnp.fl...  20.3 us
    dot_general x20, matrix products, advance(): jnp.einsum('nrs,nsu->nru', factor, 3.0 * eye_rank[None] - inner, precisio...  9.94 us
    another operation x4, other arithmetic, solve_halves(): lower = jnp.linalg.cholesky(system)  9.19 us
    reduce_sum x1, other arithmetic, group_the_sections(): return lax.all_gather(x_part, 'runs').sum(axis=0)  9.05 us
    dot_general x20, matrix products, advance(): jnp.einsum('nst,ntu->nsu', left, factor, precision=lax.Precision.HIGHEST)  8.73 us
  transfers between devices with their start and end apart: 3, of which 3 were waited for; matrix products, arithmetic and copies ran while one was open for 6% of the time, Pallas kernels for 0%

profile of v1, /device:TPU:1, one launch (start us, length us, event | category | flops | bytes accessed | tf_op | source)
XLA Modules:
  0.0 401.5 jit_solution(11531501587760731275)
XLA Ops:
  7.2 0.9 select_reduce_fusion.3
  8.1 1.1 slice_bitcast_fusion.3
  9.2 11.8 %fusion.17 = f32[8,48,512]{2,1,0:T(8,128)} fusion(bf16[8,512,2048]{2,1,0:T(8,128)(2,1)} %param.10, pred[8]{0:T(512)(128)(4,1)S(1)} %broadcast_compare_fusion, bf16[48,2048]{1,0:T(8,128)(2,1)S(1)} %get-tuple-element.81, bf16[48,2048]{1,0:T(8,128)(2,1)S(1)} %get-tuple-element.80), kind=kOutput, calls=%fused_computation.23 | convolution fusion | flops 806092800 | bytes 17956872 | tf_op jit(solution)/shard_map/nrj,nij->nri/dot_general | solution.py:25
  21.5 42.8 %all-reduce.3.cloned.1.call-done = f32[8,48,512]{2,1,0:T(8,128)} async-done(((f32[8,48,512]{2,1,0:T(8,128)}), f32[8,48,512]{2,1,0:T(8,128)}) %all-reduce.3.cloned.1.call-update) | async-done | bytes 786448 | tf_op jit(solution)/shard_map/psum | solution.py:26
  64.2 2.0 fusion.26
  66.2 0.9 select_reduce_fusion.1
  67.3 13.5 %while.22 = (s32[]{:T(128)}, f32[8,48,48]{1,2,0:T(8,128)S(1)}, f32[8,48,48]{2,1,0:T(8,128)S(1)}, s32[]{:T(128)}) while((s32[]{:T(128)}, f32[8,48,48]{1,2,0:T(8,128)S(1)}, f32[8,48,48]{2,1,0:T(8,128)S(1)}, s32[]{:T(128)}) %tuple.47), condition=%wide.region_6.7_spmd.clone, body=%wide.region_5.6_spmd.clone.sunk | while | flops 31891968 | bytes 829493 | solution.py:21
  67.8 0.4 convolution_subtract_fusion.5
  68.3 0.5 fusion.129
  69.1 0.4 convolution_subtract_fusion.5
  69.6 0.5 fusion.129
  70.5 0.4 convolution_subtract_fusion.5
  70.9 0.5 fusion.129
  71.8 0.4 convolution_subtract_fusion.5
  72.2 0.5 fusion.129
  73.1 0.4 convolution_subtract_fusion.5
  73.6 0.5 fusion.129
  74.4 0.4 convolution_subtract_fusion.5
  74.9 0.5 fusion.129
  75.8 0.4 convolution_subtract_fusion.5
  76.2 0.5 fusion.129
  77.1 0.4 convolution_subtract_fusion.5
  77.5 0.5 fusion.129
  78.4 0.4 convolution_subtract_fusion.5
  78.9 0.5 fusion.129
  79.8 0.4 convolution_subtract_fusion.5
  80.2 0.5 fusion.129
  80.7 0.8 convolution_convert_fusion.1
  81.5 8.8 %fusion.67 = f32[8,48,2048]{2,1,0:T(8,128)S(1)} fusion(bf16[8,48,512]{2,1,0:T(8,128)(2,1)S(1)} %convolution_convert_fusion.1, bf16[8,512,2048]{2,1,0:T(8,128)(2,1)} %param.10), kind=kOutput, calls=%fused_computation.103 | convolution fusion | flops 805306368 | bytes 20316160 | tf_op jit(solution)/shard_map/nsi,nij->nsj/dot_general | solution.py:33
  90.3 3.1 fusion.25
  93.4 3.3 fusion.10
  96.7 1.3 copy.34
  98.8 9.0 %custom-call.11 = f32[2,48,48]{2,1,0:T(8,128)S(1)} custom-call(f32[2,48,48]{2,1,0:T(8,128)S(1)} %fusion.51), custom_call_target="Cholesky" | custom-call | tf_op jit(solution)/shard_map/jit(cholesky)/cholesky | solution.py:42
  108.0 7.4 %custom-call.12 = f32[2,1,48,48]{2,3,1,0:T(8,128)S(1)} custom-call(f32[2,1,48,48]{3,2,1,0:T(8,128)S(1)} %select_bitcast_fusion), custom_call_target="InvertDiagBlocksLowerTriangular" | custom-call | tf_op jit(solution)/shard_map/vmap(jit(_cho_solve))/triangular_solve | solution.py:38
  115.4 189.4 %all-gather.3.cloned.1.call-done = f32[64,48,2048]{2,1,0:T(8,128)} async-done(((f32[2,48,2048]{2,1,0:T(8,128)}), f32[64,48,2048]{2,1,0:T(8,128)}) %all-gather.3.cloned.1.call-update) | async-done | bytes 25165840 | tf_op jit(solution)/shard_map/all_gather | solution.py:73
  304.9 9.0 %reduce_sum.45 = f32[2,48,2048]{2,1,0:T(8,128)S(1)} reduce(f32[32,2,48,2048]{3,2,1,0:T(8,128)} %bitcast.108, f32[]{:T(128)} %constant.79.clone.1), dimensions={0}, to_apply=%region_7.8 | reduce | flops 6094848 | bytes 25952260 | tf_op jit(solution)/shard_map/reduce_sum | solution.py:73
  313.9 0.8 fusion.48
  314.7 0.8 fusion.46
  315.6 12.1 %fusion.12 = f32[8,48,512]{2,1,0:T(8,128)} fusion(bf16[8,512,2048]{2,1,0:T(8,128)(2,1)} %param.10, f32[48,2048]{1,0:T(8,128)S(1)} %get-tuple-element.79, f32[48,2048]{1,0:T(8,128)S(1)} %get-tuple-element.78, pred[8]{0:T(512)(128)(4,1)S(1)} %broadcast_compare_fusion), kind=kOutput, calls=%fused_computation.18 | convolution fusion | flops 806092800 | bytes 18350088 | tf_op jit(solution)/shard_map/nrj,nij->nri/dot_general | solution.py:25
  327.9 4.5 %fusion.8 = f32[8,48,2048]{2,1,0:T(8,128)} fusion(f32[48,2048]{1,0:T(8,128)S(1)} %get-tuple-element.79, f32[48,2048]{1,0:T(8,128)S(1)} %get-tuple-element.78, pred[8]{0:T(512)(128)(4,1)S(1)} %broadcast_compare_fusion, f32[8,48]{1,0:T(8,128)S(1)} %fusion.56, f32[48,48]{1,0:T(8,128)S(1)} %get-tuple-element.83, f32[48,48]{1,0:T(8,128)S(1)} %get-tuple-element.82), kind=kOutput, calls=%fused_computation.12 | convolution fusion | flops 453808128 | bytes 3952136 | tf_op jit(solution)/shard_map/nrs,nsj->nrj/dot_general | solution.py:80
  332.4 33.8 %all-reduce.5.cloned.1.call-done = f32[8,48,512]{2,1,0:T(8,128)} async-done(((f32[8,48,512]{2,1,0:T(8,128)}), f32[8,48,512]{2,1,0:T(8,128)}) %all-reduce.5.cloned.1.call-update) | async-done | bytes 786448 | tf_op jit(solution)/shard_map/psum | solution.py:26
  366.2 2.0 fusion.24
  368.1 0.9 select_reduce_fusion
  369.2 13.5 %while.23 = (s32[]{:T(128)}, f32[8,48,48]{1,2,0:T(8,128)S(1)}, f32[8,48,48]{2,1,0:T(8,128)S(1)}, s32[]{:T(128)}) while((s32[]{:T(128)}, f32[8,48,48]{1,2,0:T(8,128)S(1)}, f32[8,48,48]{2,1,0:T(8,128)S(1)}, s32[]{:T(128)}) %tuple.50), condition=%wide.region_12.13_spmd.clone, body=%wide.region_11.12_spmd.clone.sunk | while | flops 31891968 | bytes 829493 | solution.py:21
  369.8 0.4 convolution_subtract_fusion.6
  370.3 0.5 fusion.138
  371.6 0.5 fusion.138
  372.5 0.4 convolution_subtract_fusion.6
  372.9 0.5 fusion.138
  373.8 0.4 convolution_subtract_fusion.6
  374.2 0.5 fusion.138
  375.1 0.4 convolution_subtract_fusion.6
  375.6 0.5 fusion.138
  376.5 0.4 convolution_subtract_fusion.6
  376.9 0.5 fusion.138
  377.8 0.4 convolution_subtract_fusion.6
  378.2 0.5 fusion.138
  379.1 0.4 convolution_subtract_fusion.6
  379.6 0.5 fusion.138
  380.4 0.4 convolution_subtract_fusion.6
  380.9 0.5 fusion.138
  382.2 0.5 fusion.138
  382.7 0.8 convolution_convert_fusion
  383.5 11.5 %convolution_subtract_fusion.2 = f32[8,48,2048]{2,1,0:T(8,128)} fusion(f32[8,48,2048]{2,1,0:T(8,128)} %fusion.8, bf16[8,48,512]{2,1,0:T(8,128)(2,1)S(1)} %convolution_convert_fusion, bf16[8,512,2048]{2,1,0:T(8,128)(2,1)} %param.10), kind=kOutput, calls=%fused_computation.17 | convolution fusion | flops 806092800 | bytes 23461888 | tf_op jit(solution)/shard_map/nsi,nij->nsj/dot_general | solution.py:33
  (99 shorter events, 9.5 us)
Async XLA Ops:
  7.2 57.1 %all-reduce.3.cloned.1.call-start = ((), (), s32[]{:S(2)}) async-start(), calls=%async_computation | async-start | bytes 1572864 | tf_op jit(solution)/shard_map/psum | solution.py:26
  9.2 12.1 %copy-start.2 = (f32[256,48]{0,1:T(8,128)S(1)}, f32[256,48]{0,1:T(8,128)}, u32[]{:S(2)}) copy-start(f32[256,48]{0,1:T(8,128)} %param.12) | copy-start | bytes 147460
  9.2 12.2 %copy-start.1 = (f32[2,48,48]{2,1,0:T(8,128)S(1)}, f32[2,48,48]{2,1,0:T(8,128)}, u32[]{:S(2)}) copy-start(f32[2,48,48]{2,1,0:T(8,128)} %param.13) | copy-start | bytes 55300
  21.1 283.8 %all-gather.3.cloned.1.call-start = ((), (), s32[]{:S(2)}) async-start(), calls=%async_computation.2 | async-start | bytes 25952256 | tf_op jit(solution)/shard_map/all_gather | solution.py:73
  93.4 4.7 %copy-start.3 = (s32[256]{0:T(256)S(1)}, s32[256]{0:T(256)}, u32[]{:S(2)}) copy-start(s32[256]{0:T(256)} %param.14) | copy-start | bytes 3076
  98.0 268.1 %all-reduce.5.cloned.1.call-start = ((), (), s32[]{:S(2)}) async-start(), calls=%async_computation.1 | async-start | bytes 1572864 | tf_op jit(solution)/shard_map/psum | solution.py:26
  315.5 12.1 %copy-start = (f32[2,48,2048]{2,1,0:T(8,128)}, f32[2,48,2048]{2,1,0:T(8,128)S(1)}, u32[]{:S(2)}) copy-start(f32[2,48,2048]{2,1,0:T(8,128)S(1)} %fusion.46) | copy-start | bytes 2359300
Sparse Core Ops, SparseCore 0:
  21.2 42.9 all-reduce.2
  98.1 206.6 all-gather.2
  327.8 38.2 all-reduce.4
